TPU v7x, 512 devices: a whole 4x8x8 slice. The times are simulated.
512 devices in a mesh: seq: 16 (over z, core), expert: 32 (over x, y).
Axes of the slice: x: 4, y: 8, z: 8, core: 2. Of those that a mesh axis runs over, the one named last changes fastest.
Arguments:
- hidden: bfloat16 [32, 1024, 2048], P('expert', 'seq'), may hold values from -6 to 6
- queries: bfloat16 [32, 1024, 4608], P('expert', 'seq'), may hold values from -5 to 5
- suffix_latent: bfloat16 [32, 1024, 576], P('expert', 'seq'), may hold values from -6 to 6
- prefix_latent: bfloat16 [2, 1024, 576], P(None, 'seq'), may hold values from -6 to 6
- lengths: int32 [32, 4], P('expert'), may hold values from 1 to 512, 1024 in all within a row
- prefix_of: int32 [32, 4], P('expert'), may hold values from 0 to 1
- value_up: bfloat16 [8, 512, 128], replicated, may hold values from -1 to 1
- out_proj: bfloat16 [1024, 2048], P(None, 'expert'), may hold values from -0.1875 to 0.1875
- norm_gain: float32 [2048], replicated, may hold values from 0.5 to 1.5
- router: bfloat16 [2048, 32], replicated, may hold values from -0.0625 to 0.0625
- routes: int32 [32, 1024, 6], P('expert', 'seq'), may hold values from 0 to 31, all different within a row; in each aligned block of 64 rows (0 to 63, 64 to 127, ..., all dimensions but the last counted through in order) at most 16 rows name the same one
- expert_in: bfloat16 [32, 2048, 1408], P('expert', 'seq'), may hold values from -0.125 to 0.125
- expert_out: bfloat16 [32, 2048, 704], P('expert', 'seq'), may hold values from -1.25 to 1.25
Outputs:
- layer_out: bfloat16 [32, 1024, 2048], P('expert', 'seq')
Inputs may be any that keep to these rules, and one draw needn't show every extreme that they name: `routes`: among the rows of one device (aligned blocks of 64 tokens) no expert is named more than 16 times, a bound that some block reaches; a token's 6 experts differ. `lengths`: each row sums to 1024; its longest request has exactly 512 tokens.
All inputs are finite; a program needn't handle non-finite values.
Results may differ from a plain program's by a relative error of at most 0.013.
Values may be sent and summed in bfloat16 or wider, within the bound.
No kernel may reach another device: no remote copies, remote signals or barrier semaphores. Data moves between devices by JAX's collectives and lax.ppermute only.
A program may use at most 128 MiB of HBM per device.

v0:
```python
import jax
import jax.numpy as jnp
from jax import lax
from jax.sharding import PartitionSpec as P

qk_scale = 192.0 ** (-0.5)
big_negative = -1e30


def request_of(positions, request_ends):
    return jnp.sum((positions[:, None] >= request_ends[None, :]).astype(jnp.int32), axis=1)


def merge_scores(running, scores, allowed, values):
    running_max, running_sum, running_acc = running
    new_max = jnp.maximum(running_max, jnp.max(jnp.where(allowed, scores, big_negative), axis=2))
    weights = jnp.where(allowed, jnp.exp(scores - new_max[:, :, None]), 0.0)
    new_sum = jnp.sum(weights, axis=2)
    new_acc = jnp.einsum(
        "thn,nl->thl", weights.astype(jnp.bfloat16), values, preferred_element_type=jnp.float32
    )
    return (new_max, new_sum, new_acc)


def local(
    hidden,
    queries,
    suffix_latent,
    prefix_latent,
    lengths,
    prefix_of,
    value_up,
    out_proj,
    norm_gain,
    router,
    routes,
    expert_in,
    expert_out,
):
    local_tokens = hidden.shape[1]
    model_width = hidden.shape[2]
    key_width = suffix_latent.shape[2]
    head_count = value_up.shape[0]
    latent_width = value_up.shape[1]
    expert_count = router.shape[1]
    top_count = routes.shape[2]
    capacity = 4 * local_tokens * top_count // (3 * expert_count)
    request_count = lengths.shape[1]
    request_ends = jnp.cumsum(lengths[0])
    my_positions = lax.axis_index("seq") * local_tokens + jnp.arange(local_tokens, dtype=jnp.int32)
    my_requests = request_of(my_positions, request_ends)
    request_ids = jnp.arange(request_count, dtype=jnp.int32)
    chosen = jnp.sum(
        jnp.where(my_requests[:, None] == request_ids[None, :], prefix_of[0][None, :], 0), axis=1
    )
    prefix_pick = chosen[:, None] == jnp.arange(2, dtype=jnp.int32)[None, :]
    single_prefix = jnp.all(chosen == chosen[0])
    my_prefix = chosen[0]
    query_rows = queries[0].reshape(local_tokens, head_count, key_width)
    start_state = (
        jnp.full((local_tokens, head_count), big_negative, jnp.float32),
        jnp.zeros((local_tokens, head_count), jnp.float32),
        jnp.zeros((local_tokens, head_count, latent_width), jnp.float32),
    )
    suffix_piece = lax.all_gather(suffix_latent, "seq", axis=1, tiled=True)
    prefix_piece = lax.all_gather(prefix_latent, "seq", axis=1, tiled=True)
    piece_rows = suffix_piece.shape[1]
    suffix_keys = suffix_piece[0]
    key_positions = jnp.arange(piece_rows, dtype=jnp.int32)
    key_requests = request_of(key_positions, request_ends)
    suffix_allowed = (key_requests[None, :] == my_requests[:, None]) & (
        key_positions[None, :] <= my_positions[:, None]
    )
    suffix_scores = (
        jnp.einsum("thk,nk->thn", query_rows, suffix_keys, preferred_element_type=jnp.float32)
        * qk_scale
    )

    def one_prefix(running_state):
        chosen_keys = lax.dynamic_index_in_dim(prefix_piece, my_prefix, 0, keepdims=False)
        prefix_scores = (
            jnp.einsum("thk,nk->thn", query_rows, chosen_keys, preferred_element_type=jnp.float32)
            * qk_scale
        )
        scores = jnp.concatenate([suffix_scores, prefix_scores], axis=2)
        every_key = jnp.ones((local_tokens, piece_rows), dtype=bool)
        allowed = jnp.concatenate([suffix_allowed, every_key], axis=1)[:, None, :]
        values = jnp.concatenate(
            [suffix_keys[:, :latent_width], chosen_keys[:, :latent_width]], axis=0
        )
        return merge_scores(running_state, scores, allowed, values)

    def two_prefixes(running_state):
        prefix_scores = (
            jnp.einsum(
                "thk,pnk->thpn", query_rows, prefix_piece, preferred_element_type=jnp.float32
            )
            * qk_scale
        )
        scores = jnp.concatenate(
            [suffix_scores, prefix_scores.reshape(local_tokens, head_count, 2 * piece_rows)], axis=2
        )
        prefix_allowed = jnp.broadcast_to(
            prefix_pick[:, :, None], (local_tokens, 2, piece_rows)
        ).reshape(local_tokens, 2 * piece_rows)
        allowed = jnp.concatenate([suffix_allowed, prefix_allowed], axis=1)[:, None, :]
        values = jnp.concatenate(
            [
                suffix_keys[:, :latent_width],
                prefix_piece[:, :, :latent_width].reshape(2 * piece_rows, latent_width),
            ],
            axis=0,
        )
        return merge_scores(running_state, scores, allowed, values)

    final_max, final_sum, final_acc = lax.cond(single_prefix, one_prefix, two_prefixes, start_state)
    latent_out = (final_acc / final_sum[:, :, None]).astype(jnp.bfloat16)
    value_out = jnp.einsum(
        "thl,hlv->thv", latent_out, value_up, preferred_element_type=jnp.float32
    ).astype(jnp.bfloat16)
    value_out = value_out.reshape(local_tokens, head_count * value_up.shape[2])
    projected = jnp.dot(
        value_out,
        lax.all_gather(out_proj, "expert", axis=1, tiled=True),
        preferred_element_type=jnp.float32,
    )
    residual = hidden[0].astype(jnp.float32) + projected
    normed = (
        residual
        * lax.rsqrt(jnp.mean(residual * residual, axis=1, keepdims=True) + 1e-06)
        * norm_gain
    ).astype(jnp.bfloat16)
    logits = jnp.dot(normed, router, preferred_element_type=jnp.float32)
    expert_probs = jax.nn.softmax(logits, axis=1)
    expert_ids = jnp.arange(expert_count, dtype=jnp.int32)
    my_routes = routes[0]
    matches = my_routes[:, :, None] == expert_ids[None, None, :]
    gate_values = jnp.sum(jnp.where(matches, expert_probs[:, None, :], 0.0), axis=2)
    flat_hits = matches.reshape(local_tokens * top_count, expert_count).astype(jnp.int32)
    earlier = jnp.cumsum(flat_hits, axis=0) - flat_hits
    slot_index = jnp.sum(earlier * flat_hits, axis=1).reshape(local_tokens, top_count)
    cell_index = my_routes * capacity + slot_index
    cell_ids = jnp.arange(expert_count * capacity, dtype=jnp.int32)
    placing = jnp.sum(
        (cell_ids[:, None, None] == cell_index[None, :, :]).astype(jnp.int32), axis=2
    ).astype(jnp.bfloat16)
    outgoing = jnp.dot(placing, normed, preferred_element_type=jnp.float32).astype(jnp.bfloat16)
    outgoing = outgoing.reshape(expert_count, capacity, model_width)
    incoming = lax.all_to_all(outgoing, "expert", split_axis=0, concat_axis=0, tiled=True)
    full_in, full_out = (
        lax.all_gather(expert_in, "seq", axis=1, tiled=True),
        lax.all_gather(expert_out, "seq", axis=1, tiled=True),
    )
    all_rows = incoming.reshape(-1, model_width)
    gate_up = jnp.dot(all_rows, full_in[0], preferred_element_type=jnp.float32)
    hidden_units = gate_up.shape[1] // 2
    active = (jax.nn.silu(gate_up[:, :hidden_units]) * gate_up[:, hidden_units:]).astype(
        jnp.bfloat16
    )
    produced = lax.dot_general(
        active, full_out[0], (((1,), (1,)), ((), ())), preferred_element_type=jnp.float32
    ).astype(jnp.bfloat16)
    returned = lax.all_to_all(
        produced.reshape(-1, capacity, model_width),
        "expert",
        split_axis=0,
        concat_axis=0,
        tiled=True,
    )
    returned_rows = returned.reshape(-1, model_width)
    picked = returned_rows[cell_index]
    routed_sum = jnp.sum(gate_values[:, :, None] * picked.astype(jnp.float32), axis=1)
    layer_out = (residual + routed_sum).astype(jnp.bfloat16)
    return layer_out[None]


def solution(mesh):
    in_specs = (
        P("expert", "seq", None),
        P("expert", "seq", None),
        P("expert", "seq", None),
        P(None, "seq", None),
        P("expert", None),
        P("expert", None),
        P(),
        P(None, "expert"),
        P(),
        P(),
        P("expert", "seq", None),
        P("expert", "seq", None),
        P("expert", "seq", None),
    )
    out_specs = P("expert", "seq", None)
    return jax.shard_map(local, mesh=mesh, in_specs=in_specs, out_specs=out_specs, check_vma=False)
```

profile of v0, /device:TPU:16, one launch (start us, length us, event | category | flops | bytes accessed | tf_op | source)
XLA Modules:
  0.0 368.0 jit_solution(16596417180253832410)
XLA Ops:
  7.3 1.8 copy.86
  13.9 2.4 reshape_squeeze.3
  20.0 36.3 %all-gather.8.cloned.1.call-done = bf16[1,1024,576]{2,1,0:T(8,128)(2,1)} async-done(((bf16[1,64,576]{2,1,0:T(8,128)(2,1)}), bf16[1,1024,576]{2,1,0:T(8,128)(2,1)}) %all-gather.8.cloned.1.call-update) | async-done | bytes 1179664 | tf_op jit(solution)/shard_map/all_gather | solution.py:65
  56.3 2.4 copy.87
  58.7 2.5 convolution_multiply_fusion
  61.3 39.0 %all-gather.6.cloned.1.call-done = bf16[2,1024,576]{2,0,1:T(2,128)(2,1)} async-done(((bf16[2,64,576]{2,0,1:T(2,128)(2,1)}), bf16[2,1024,576]{2,0,1:T(2,128)(2,1)}) %all-gather.6.cloned.1.call-update) | async-done | bytes 2359312 | tf_op jit(solution)/shard_map/all_gather | solution.py:66
  100.3 31.3 %conditional.1 = (f32[64,8,512]{2,1,0:T(8,128)}, f32[64,8]{1,0:T(8,128)S(1)}) conditional(s32[]{:T(128)} %convert_element_type.64, (s32[64]{0:T(128)S(1)}, s32[64,2]{1,0:T(8,128)S(1)}, pred[64,1024]{1,0:T(8,128)(4,1)S(1)}, bf16[64,8,576]{2,1,0:T(8,128)(2,1)}, bf16[2,1024,576]{2,0,1:T(2,128)(2,1)}, /*index=5*/f32[64,8,1024]{2,1,0:T(8,128)S(1)}, ...), branch_computations={%region_5.8_spmd, %region_8.11_spmd} | conditional | flops 2843409920 | bytes 92157032 | solution.py:116
  100.3 7.4 %copy.88 = bf16[2,1024,576]{1,2,0:T(8,128)(2,1)} copy(bf16[2,1024,576]{2,0,1:T(2,128)(2,1)} %get-tuple-element.110) | data formatting | bytes 4718592 | tf_op jit(solution)/shard_map
  107.6 3.7 fusion.10
  111.7 1.2 select_reduce_fusion
  114.5 1.5 slice.36
  116.0 4.0 %copy.82 = bf16[2,1024,512]{2,1,0:T(8,128)(2,1)} copy(bf16[2,1024,512]{1,2,0:T(8,128)(2,1)} %slice.36) | data formatting | bytes 4194304 | tf_op jit(solution)/shard_map/cond/branch_0_fun/slice | solution.py:110
  120.0 2.4 copy.89
  122.4 1.3 slice.35
  123.7 5.9 %fusion.2 = f32[64,8,512]{2,1,0:T(8,128)} fusion(bf16[2048,512]{1,0:T(8,128)(2,1)} %bitcast.104, bf16[1024,512]{1,0:T(8,128)(2,1)S(1)} %slice.35, f32[64,8,2048]{2,1,0:T(8,128)} %bitcast.98, f32[64,8,1024]{2,1,0:T(8,128)S(1)} %get-tuple-element.36, f32[64,8]{1,0:T(8,128)S(1)} %broadcast_maximum_fusion, pred[64,3072]{1,0:T(8,128)(4,1)S(1)} %pad_add_fusion), kind=kOutput, calls=%fused_computation.7 | convolution fusion | flops 1623195648 | bytes 10684416 | tf_op jit(solution)/shard_map/cond/branch_0_fun/thn,nl->thl/dot_general | solution.py:19
  129.6 1.8 fusion.1
  131.5 1.4 divide_convert_fusion
  133.4 54.2 %all-gather.10.cloned.1.call-done = bf16[1024,2048]{0,1:T(8,128)(2,1)} async-done(((bf16[1024,64]{0,1:T(8,128)(2,1)}), bf16[1024,2048]{0,1:T(8,128)(2,1)}) %all-gather.10.cloned.1.call-update) | async-done | bytes 4194320 | tf_op jit(solution)/shard_map/all_gather | solution.py:124
  187.6 3.7 %multiply_reduce_fusion.1 = (f32[64]{0:T(128)S(1)}, f32[64,2048]{1,0:T(8,128)S(1)}) fusion(bf16[1024,2048]{0,1:T(8,128)(2,1)} %all-gather.10.cloned.1.call-done, bf16[8,8,8,128]{3,2,1,0:T(8,128)(2,1)S(1)} %fusion.33, bf16[1,64,2048]{2,1,0:T(8,128)(2,1)S(1)} %copy-done.9), kind=kOutput, calls=%fused_computation.60 | convolution fusion | flops 268959680 | bytes 5112064 | tf_op jit(solution)/shard_map/dot_general | solution.py:122
  192.1 2.1 convolution_convert_fusion.1
  194.1 7.2 %all-to-all-start = ((bf16[32,16,2048]{2,1,0:T(8,128)(2,1)}), bf16[32,16,2048]{2,1,0:T(8,128)(2,1)S(1)}, u32[]{:S(2)}, u32[]{:S(2)}) async-start(bf16[32,16,2048]{2,1,0:T(8,128)(2,1)} %bitcast.20), calls=%async_computation | async-start | bytes 4194304 | tf_op jit(solution)/shard_map/all_to_all | solution.py:149
  201.3 34.9 %all-gather.12.cloned.1.call-done = bf16[1,2048,1408]{2,1,0:T(8,128)(2,1)} async-done(((bf16[1,128,1408]{2,1,0:T(8,128)(2,1)}), bf16[1,2048,1408]{2,1,0:T(8,128)(2,1)}) %all-gather.12.cloned.1.call-update) | async-done | bytes 5767184 | tf_op jit(solution)/shard_map/all_gather | solution.py:151
  236.2 11.3 %all-to-all-done = bf16[32,16,2048]{2,1,0:T(8,128)(2,1)S(1)} async-done(((bf16[32,16,2048]{2,1,0:T(8,128)(2,1)}), bf16[32,16,2048]{2,1,0:T(8,128)(2,1)S(1)}, u32[]{:S(2)}, u32[]{:S(2)}) %all-to-all-start) | async-done | bytes 2097184 | tf_op jit(solution)/shard_map/all_to_all | solution.py:149
  247.5 7.6 %fusion.28 = f32[512,1408]{1,0:T(8,128)} fusion(bf16[512,2048]{1,0:T(8,128)(2,1)S(1)} %bitcast.103, bf16[1,2048,1408]{2,1,0:T(8,128)(2,1)} %all-gather.12.cloned.1.call-done), kind=kOutput, calls=%fused_computation.40 | convolution fusion | flops 2952790016 | bytes 10747904 | tf_op jit(solution)/shard_map/dot_general | solution.py:155
  255.2 28.3 %all-gather.14.cloned.1.call-done = bf16[1,2048,704]{1,2,0:T(8,128)(2,1)} async-done(((bf16[1,128,704]{1,2,0:T(8,128)(2,1)}), bf16[1,2048,704]{1,2,0:T(8,128)(2,1)}) %all-gather.14.cloned.1.call-update) | async-done | bytes 2883600 | tf_op jit(solution)/shard_map/all_gather | solution.py:152
  283.5 6.0 %convolution_convert_fusion = bf16[512,2048]{1,0:T(8,128)(2,1)} fusion(bf16[1,2048,704]{1,2,0:T(8,128)(2,1)} %all-gather.14.cloned.1.call-done, f32[512,1408]{1,0:T(8,128)} %fusion.28), kind=kOutput, calls=%fused_computation.43 | convolution fusion | flops 1479606272 | bytes 8126464 | tf_op jit(solution)/shard_map/dot_general | solution.py:160
  289.5 10.0 %all-to-all-start.1 = ((bf16[32,16,2048]{2,1,0:T(8,128)(2,1)}), bf16[32,16,2048]{2,1,0:T(8,128)(2,1)S(1)}, u32[]{:S(2)}, u32[]{:S(2)}) async-start(bf16[32,16,2048]{2,1,0:T(8,128)(2,1)} %bitcast.102), calls=%async_computation.1 | async-start | bytes 4194304 | tf_op jit(solution)/shard_map/all_to_all | solution.py:163
  299.8 1.3 fusion.50
  301.3 48.6 %all-to-all-done.1 = bf16[32,16,2048]{2,1,0:T(8,128)(2,1)S(1)} async-done(((bf16[32,16,2048]{2,1,0:T(8,128)(2,1)}), bf16[32,16,2048]{2,1,0:T(8,128)(2,1)S(1)}, u32[]{:S(2)}, u32[]{:S(2)}) %all-to-all-start.1) | async-done | bytes 2097184 | tf_op jit(solution)/shard_map/all_to_all | solution.py:163
  349.9 3.1 gather_fusion
  353.0 3.9 %reshape.155 = f32[64,6,2048]{2,1,0:T(8,128)} reshape(bf16[384,2048]{1,0:T(8,128)(2,1)} %gather_fusion) | data formatting | bytes 4718592 | tf_op jit(solution)/shard_map/convert_element_type | solution.py:172
  356.9 3.8 %multiply_reduce_fusion = f32[64,2048]{1,0:T(8,128)S(1)} fusion(f32[64,6,2048]{2,1,0:T(8,128)} %reshape.155, f32[64,6]{1,0:T(8,128)S(1)} %copy.96), kind=kLoop, calls=%fused_computation.42 | loop fusion | flops 1441792 | bytes 3671552 | tf_op jit(solution)/shard_map/reduce_sum | solution.py:172
  (69 shorter events, 12.9 us)
Async XLA Ops:
  6.5 126.4 %copy-start = (bf16[8,512,128]{2,1,0:T(8,128)(2,1)S(1)}, bf16[8,512,128]{2,1,0:T(8,128)(2,1)}, u32[]{:S(2)}) copy-start(bf16[8,512,128]{2,1,0:T(8,128)(2,1)} %param.21) | copy-start | bytes 3145732
  6.5 49.8 %all-gather.8.cloned.1.call-start = ((), (), s32[]{:S(2)}) async-start(), calls=%async_computation.3 | async-start | bytes 1392640 | tf_op jit(solution)/shard_map/all_gather | solution.py:65
  7.3 93.0 %all-gather.6.cloned.1.call-start = ((), (), s32[]{:S(2)}) async-start(), calls=%async_computation.2 | async-start | bytes 2785280 | tf_op jit(solution)/shard_map/all_gather | solution.py:66
  9.1 178.5 %all-gather.10.cloned.1.call-start = ((), (), s32[]{:S(2)}) async-start(), calls=%async_computation.4 | async-start | bytes 4325376 | tf_op jit(solution)/shard_map/all_gather | solution.py:124
  9.8 226.4 %all-gather.12.cloned.1.call-start = ((), (), s32[]{:S(2)}) async-start(), calls=%async_computation.5 | async-start | bytes 6127616 | tf_op jit(solution)/shard_map/all_gather | solution.py:151
  10.4 273.1 %all-gather.14.cloned.1.call-start = ((), (), s32[]{:S(2)}) async-start(), calls=%async_computation.6 | async-start | bytes 3063808 | tf_op jit(solution)/shard_map/all_gather | solution.py:152
  111.3 2.1 copy-start.1
  111.7 2.7 copy-start.4
  123.7 5.9 %copy-start.2 = (f32[64,8,2,1024]{3,1,2,0:T(8,128)S(1)}, f32[64,8,2,1024]{3,1,2,0:T(8,128)}, u32[]{:S(2)}) copy-start(f32[64,8,2,1024]{3,1,2,0:T(8,128)} %copy-done.1) | copy-start | bytes 12582916 | tf_op jit(solution)/shard_map/cond
  131.5 56.0 %copy-start.9 = (bf16[1,64,2048]{2,1,0:T(8,128)(2,1)S(1)}, bf16[1,64,2048]{2,1,0:T(8,128)(2,1)}, u32[]{:S(2)}) copy-start(bf16[1,64,2048]{2,1,0:T(8,128)(2,1)} %param.15) | copy-start | bytes 786436
  133.3 58.7 %copy-start.8 = (s32[512,64]{0,1:T(8,128)S(1)}, s32[512,64]{0,1:T(8,128)}, u32[]{:S(2)}) copy-start(s32[512,64]{0,1:T(8,128)} %convert_reduce_fusion) | copy-start | bytes 393220
  133.3 58.7 %copy-start.11 = (f32[2048]{0:T(1024)S(1)}, f32[2048]{0:T(1024)}, u32[]{:S(2)}) copy-start(f32[2048]{0:T(1024)} %param.23) | copy-start | bytes 24580
  191.2 0.8 copy-start.5
  194.1 53.4 %all-to-all-start = ((bf16[32,16,2048]{2,1,0:T(8,128)(2,1)}), bf16[32,16,2048]{2,1,0:T(8,128)(2,1)S(1)}, u32[]{:S(2)}, u32[]{:S(2)}) async-start(bf16[32,16,2048]{2,1,0:T(8,128)(2,1)} %bitcast.20), calls=%async_computation | async-start | bytes 4194304 | tf_op jit(solution)/shard_map/all_to_all | solution.py:149
  289.5 10.0 %copy-start.12 = (s32[1,64,6]{1,0,2:T(1,128)S(1)}, s32[1,64,6]{1,0,2:T(1,128)}, u32[]{:S(2)}) copy-start(s32[1,64,6]{1,0,2:T(1,128)} %param.25) | copy-start | bytes 4612
  289.5 10.3 %copy-start.10 = (bf16[2048,32]{0,1:T(8,128)(2,1)S(1)}, bf16[2048,32]{0,1:T(8,128)(2,1)}, u32[]{:S(2)}) copy-start(bf16[2048,32]{0,1:T(8,128)(2,1)} %param.24) | copy-start | bytes 393220
  289.5 60.4 %all-to-all-start.1 = ((bf16[32,16,2048]{2,1,0:T(8,128)(2,1)}), bf16[32,16,2048]{2,1,0:T(8,128)(2,1)S(1)}, u32[]{:S(2)}, u32[]{:S(2)}) async-start(bf16[32,16,2048]{2,1,0:T(8,128)(2,1)} %bitcast.102), calls=%async_computation.1 | async-start | bytes 4194304 | tf_op jit(solution)/shard_map/all_to_all | solution.py:163
  356.9 3.8 %copy-start.6 = (f32[64,2048]{1,0:T(8,128)S(1)}, f32[64,2048]{1,0:T(8,128)}, u32[]{:S(2)}) copy-start(f32[64,2048]{1,0:T(8,128)} %copy-done.5) | copy-start | bytes 1572868
Sparse Core Ops, SparseCore 0:
  9.5 46.7 all-gather.7
  58.4 41.7 all-gather.5
  103.4 84.0 all-gather.9
  189.5 46.6 all-gather.11
  238.1 45.3 all-gather.13
where the time goes:
time: 369 us; the launch traced here: 368 us
  waiting for transfers between devices  255 us (69%)
  local copies, waits for them, and re-layouts  34.7 us (9%)
  matrix products  33.2 us (9%)
  starting transfers between devices  17.3 us (5%)
  between operations  14 us (4%)
  other arithmetic  13.5 us (4%)
    all_gather x1, waiting for transfers between devices, local(): lax.all_gather(out_proj, 'expert', axis=1, tiled=True)  54.2 us
    all_to_all x1, waiting for transfers between devices, local(): lax.all_to_all(produced.reshape(-1, capacity, model_width), 'expert', spl...  48.6 us
    all_gather x1, waiting for transfers between devices, local(): prefix_piece = lax.all_gather(prefix_latent, 'seq', axis=1, tiled=True)  39 us
    all_gather x1, waiting for transfers between devices, local(): suffix_piece = lax.all_gather(suffix_latent, 'seq', axis=1, tiled=True)  36.3 us
    all_gather x1, waiting for transfers between devices, local(): lax.all_gather(expert_in, 'seq', axis=1, tiled=True)  34.9 us
    all_gather x1, waiting for transfers between devices, local(): lax.all_gather(expert_out, 'seq', axis=1, tiled=True)  28.3 us
    all_to_all x1, waiting for transfers between devices, local(): lax.all_to_all(outgoing, 'expert', split_axis=0, concat_axis=0, tiled=True)  11.3 us
    all_to_all x1, starting transfers between devices, local(): lax.all_to_all(produced.reshape(-1, capacity, model_width), 'expert', spl...  9.96 us
  transfers between devices with their start and end apart: 7, of which 7 were waited for; matrix products, arithmetic and copies ran while one was open for 17% of the time, Pallas kernels for 0%

commit v1 on v0

--- a/solution.py
+++ b/solution.py
@@ -5,6 +5,18 @@
 
 qk_scale = 192.0 ** (-0.5)
 big_negative = -1e30
+
+
+def _prepare_words(tile_in):
+    return jnp.concatenate(
+        lax.all_to_all(
+            jnp.stack(lax.axis_size("seq") * [tile_in], axis=0),
+            axis_name="seq",
+            split_axis=0,
+            concat_axis=0,
+        ),
+        1,
+    )
 
 
 def request_of(positions, request_ends):
@@ -148,7 +160,7 @@
     outgoing = outgoing.reshape(expert_count, capacity, model_width)
     incoming = lax.all_to_all(outgoing, "expert", split_axis=0, concat_axis=0, tiled=True)
     full_in, full_out = (
-        lax.all_gather(expert_in, "seq", axis=1, tiled=True),
+        _prepare_words(expert_in),
         lax.all_gather(expert_out, "seq", axis=1, tiled=True),
     )
     all_rows = incoming.reshape(-1, model_width)

time: 369 us -> 402 us (1.089)
  the two profiles are of different devices: /device:TPU:16 before, /device:TPU:8 now
where the time goes in v1:
time: 402 us; the launch traced here: 401 us
  waiting for transfers between devices  250 us (62%)
  blocking collectives  53.7 us (13%)
  local copies, waits for them, and re-layouts  28.9 us (7%)
  matrix products  27.3 us (7%)
  starting transfers between devices  16 us (4%)
  between operations  14.1 us (4%)
  other arithmetic  10.8 us (3%)
    all_gather x1, waiting for transfers between devices, local(): prefix_piece = lax.all_gather(prefix_latent, 'seq', axis=1, tiled=True)  86.6 us
    all_gather x1, waiting for transfers between devices, local(): lax.all_gather(out_proj, 'expert', axis=1, tiled=True)  71.1 us
    all_to_all x1, blocking collectives, local(): lax.all_to_all(outgoing, 'expert', split_axis=0, concat_axis=0, tiled=True)  53.7 us
    all_gather x1, waiting for transfers between devices, local(): suffix_piece = lax.all_gather(suffix_latent, 'seq', axis=1, tiled=True)  45.7 us
    all_to_all x1, waiting for transfers between devices, local(): lax.all_to_all(produced.reshape(-1, capacity, model_width), 'expert', spl...  44.7 us
    all_to_all x1, starting transfers between devices, _prepare_words(): lax.all_to_all(jnp.stack(lax.axis_size('seq') * [tile_in], axis=0), axis_...  10.6 us
    another operation x2, local copies, waits for them, and re-layouts  8.61 us
  transfers between devices with their start and end apart: 6, of which 4 were waited for; matrix products, arithmetic and copies ran while one was open for 12% of the time, Pallas kernels for 0%

profile of v1, /device:TPU:8, one launch (start us, length us, event | category | flops | bytes accessed | tf_op | source)
XLA Modules:
  0.0 400.9 jit_solution(3850177149839160743)
XLA Ops:
  7.3 1.8 copy.86
  9.8 4.2 %stack.2 = bf16[16,1,128,1408]{3,2,1,0:T(8,128)(2,1)} broadcast(bf16[128,1408]{1,0:T(8,128)(2,1)} %bitcast.108), dimensions={2,3} | broadcast | bytes 6127616 | tf_op jit(solution)/shard_map/stack | solution.py:13
  14.0 10.6 %all-to-all-start.1 = ((bf16[16,1,128,1408]{3,2,1,0:T(8,128)(2,1)}), bf16[16,1,128,1408]{3,2,1,0:T(8,128)(2,1)}, u32[]{:S(2)}, u32[]{:S(2)}) async-start(bf16[16,1,128,1408]{3,2,1,0:T(8,128)(2,1)} %stack.2), calls=%async_computation.1 | async-start | bytes 11534336 | tf_op jit(solution)/shard_map/all_to_all | solution.py:12
  25.6 1.4 reshape_squeeze.3
  27.3 0.8 compare_reduce_fusion
  28.8 0.9 reduce-window.19
  30.3 0.8 convert_reduce_fusion
  31.2 45.7 %all-gather.7.cloned.1.call-done = bf16[1,1024,576]{2,1,0:T(8,128)(2,1)} async-done(((bf16[1,64,576]{2,1,0:T(8,128)(2,1)}), bf16[1,1024,576]{2,1,0:T(8,128)(2,1)}) %all-gather.7.cloned.1.call-update) | async-done | bytes 1179664 | tf_op jit(solution)/shard_map/all_gather | solution.py:77
  76.9 2.4 copy.87
  79.3 2.5 convolution_multiply_fusion
  81.9 86.6 %all-gather.5.cloned.1.call-done = bf16[2,1024,576]{2,0,1:T(2,128)(2,1)} async-done(((bf16[2,64,576]{2,0,1:T(2,128)(2,1)}), bf16[2,1024,576]{2,0,1:T(2,128)(2,1)}) %all-gather.5.cloned.1.call-update) | async-done | bytes 2359312 | tf_op jit(solution)/shard_map/all_gather | solution.py:78
  168.4 16.9 %conditional.1 = (f32[64,8,512]{2,1,0:T(8,128)}, f32[64,8]{1,0:T(8,128)S(1)}) conditional(s32[]{:T(128)} %convert_element_type.64, (s32[64]{0:T(128)S(1)}, s32[64,2]{1,0:T(8,128)S(1)}, pred[64,1024]{1,0:T(8,128)(4,1)S(1)}, bf16[64,8,576]{2,1,0:T(8,128)(2,1)}, bf16[2,1024,576]{2,0,1:T(2,128)(2,1)}, /*index=5*/f32[64,8,1024]{2,1,0:T(8,128)S(1)}, ...), branch_computations={%region_5.8_spmd, %region_8.11_spmd} | conditional | flops 2843409920 | bytes 92157032 | solution.py:128
  168.6 7.4 %copy.90 = bf16[2,1024,576]{1,2,0:T(8,128)(2,1)} copy(bf16[2,1024,576]{2,0,1:T(2,128)(2,1)} %get-tuple-element.115) | data formatting | bytes 4718592 | tf_op jit(solution)/shard_map
  176.0 2.4 multiply_bitcast_fusion
  178.4 1.2 copy.92
  180.2 1.0 fusion.18
  182.7 2.5 fusion.19
  185.4 1.4 divide_convert_fusion
  187.2 71.1 %all-gather.9.cloned.1.call-done = bf16[1024,2048]{0,1:T(8,128)(2,1)} async-done(((bf16[1024,64]{0,1:T(8,128)(2,1)}), bf16[1024,2048]{0,1:T(8,128)(2,1)}) %all-gather.9.cloned.1.call-update) | async-done | bytes 4194320 | tf_op jit(solution)/shard_map/all_gather | solution.py:136
  258.3 3.7 multiply_reduce_fusion.1
  262.0 0.8 copy-done.5
  262.8 0.8 convolution_convert_fusion.1
  263.6 53.7 %all_to_all.15 = bf16[32,16,2048]{2,1,0:T(8,128)(2,1)S(1)} all-to-all(bf16[32,16,2048]{2,1,0:T(8,128)(2,1)S(1)} %bitcast.102), channel_id=1, replica_groups=mesh['seq'=16,'expert'=32] {'expert'}, dimensions={0} | all-to-all | bytes 4194304 | tf_op jit(solution)/shard_map/all_to_all | solution.py:161
  317.3 7.6 %fusion.49 = f32[512,1408]{1,0:T(8,128)} fusion(bf16[512,2048]{1,0:T(8,128)(2,1)S(1)} %bitcast.105, bf16[2048,1408]{1,0:T(8,128)(2,1)} %bitcast.23), kind=kOutput, calls=%fused_computation.95 | convolution fusion | flops 2952790016 | bytes 10747904 | tf_op jit(solution)/shard_map/dot_general | solution.py:167
  324.9 6.0 %convolution_convert_fusion = bf16[512,2048]{1,0:T(8,128)(2,1)} fusion(bf16[1,2048,704]{1,2,0:T(8,128)(2,1)} %all-gather.11.cloned.1.call-done, f32[512,1408]{1,0:T(8,128)} %fusion.49), kind=kOutput, calls=%fused_computation.41 | convolution fusion | flops 1479606272 | bytes 8126464 | tf_op jit(solution)/shard_map/dot_general | solution.py:172
  330.9 5.3 %all-to-all-start.2 = ((bf16[32,16,2048]{2,1,0:T(8,128)(2,1)}), bf16[32,16,2048]{2,1,0:T(8,128)(2,1)S(1)}, u32[]{:S(2)}, u32[]{:S(2)}) async-start(bf16[32,16,2048]{2,1,0:T(8,128)(2,1)} %bitcast.103), calls=%async_computation.2 | async-start | bytes 4194304 | tf_op jit(solution)/shard_map/all_to_all | solution.py:175
  336.5 1.3 fusion.48
  338.1 44.7 %all-to-all-done.2 = bf16[32,16,2048]{2,1,0:T(8,128)(2,1)S(1)} async-done(((bf16[32,16,2048]{2,1,0:T(8,128)(2,1)}), bf16[32,16,2048]{2,1,0:T(8,128)(2,1)S(1)}, u32[]{:S(2)}, u32[]{:S(2)}) %all-to-all-start.2) | async-done | bytes 2097184 | tf_op jit(solution)/shard_map/all_to_all | solution.py:175
  382.8 3.1 gather_fusion
  385.9 3.9 reshape.158
  389.8 3.8 multiply_reduce_fusion
  393.6 0.8 fusion.35
  (70 shorter events, 6.6 us)
Async XLA Ops:
  6.5 180.3 %copy-start = (bf16[8,512,128]{2,1,0:T(8,128)(2,1)S(1)}, bf16[8,512,128]{2,1,0:T(8,128)(2,1)}, u32[]{:S(2)}) copy-start(bf16[8,512,128]{2,1,0:T(8,128)(2,1)} %param.21) | copy-start | bytes 3145732
  6.5 70.4 %all-gather.7.cloned.1.call-start = ((), (), s32[]{:S(2)}) async-start(), calls=%async_computation.4 | async-start | bytes 1392640 | tf_op jit(solution)/shard_map/all_gather | solution.py:77
  7.3 161.2 %all-gather.5.cloned.1.call-start = ((), (), s32[]{:S(2)}) async-start(), calls=%async_computation.3 | async-start | bytes 2785280 | tf_op jit(solution)/shard_map/all_gather | solution.py:78
  9.1 249.2 %all-gather.9.cloned.1.call-start = ((), (), s32[]{:S(2)}) async-start(), calls=%async_computation.5 | async-start | bytes 4325376 | tf_op jit(solution)/shard_map/all_gather | solution.py:136
  14.0 11.2 %copy-start.13 = (s32[1,64,6]{1,0,2:T(1,128)S(1)}, s32[1,64,6]{1,0,2:T(1,128)}, u32[]{:S(2)}) copy-start(s32[1,64,6]{1,0,2:T(1,128)} %param.25) | copy-start | bytes 4612
  14.0 11.6 %copy-start.8 = (bf16[1,64,4608]{2,1,0:T(8,128)(2,1)S(1)}, bf16[1,64,4608]{2,1,0:T(8,128)(2,1)}, u32[]{:S(2)}) copy-start(bf16[1,64,4608]{2,1,0:T(8,128)(2,1)} %param.16) | copy-start | bytes 1769476
  14.0 13.0 %copy-start.14 = (s32[1,4]{1,0:T(1,128)S(1)}, s32[1,4]{1,0:T(1,128)}, u32[]{:S(2)}) copy-start(s32[1,4]{1,0:T(1,128)} %param.19) | copy-start | bytes 52
  14.0 13.2 %copy-start.15 = (s32[1,4]{1,0:T(1,128)S(1)}, s32[1,4]{1,0:T(1,128)}, u32[]{:S(2)}) copy-start(s32[1,4]{1,0:T(1,128)} %param.20) | copy-start | bytes 52
  14.0 249.6 %all-to-all-start.1 = ((bf16[16,1,128,1408]{3,2,1,0:T(8,128)(2,1)}), bf16[16,1,128,1408]{3,2,1,0:T(8,128)(2,1)}, u32[]{:S(2)}, u32[]{:S(2)}) async-start(bf16[16,1,128,1408]{3,2,1,0:T(8,128)(2,1)} %stack.2), calls=%async_computation.1 | async-start | bytes 11534336 | tf_op jit(solution)/shard_map/all_to_all | solution.py:12
  24.6 300.3 %all-gather.11.cloned.1.call-start = ((), (), s32[]{:S(2)}) async-start(), calls=%async_computation.6 | async-start | bytes 3063808 | tf_op jit(solution)/shard_map/all_gather | solution.py:164
  180.2 1.7 copy-start.7
  181.2 1.4 copy-start.3
  185.4 73.0 %copy-start.10 = (bf16[1,64,2048]{2,1,0:T(8,128)(2,1)S(1)}, bf16[1,64,2048]{2,1,0:T(8,128)(2,1)}, u32[]{:S(2)}) copy-start(bf16[1,64,2048]{2,1,0:T(8,128)(2,1)} %param.15) | copy-start | bytes 786436
  187.2 75.6 %copy-start.9 = (s32[512,64]{0,1:T(8,128)S(1)}, s32[512,64]{0,1:T(8,128)}, u32[]{:S(2)}) copy-start(s32[512,64]{0,1:T(8,128)} %convert_reduce_fusion) | copy-start | bytes 393220
  187.2 75.6 %copy-start.12 = (f32[2048]{0:T(1024)S(1)}, f32[2048]{0:T(1024)}, u32[]{:S(2)}) copy-start(f32[2048]{0:T(1024)} %param.23) | copy-start | bytes 24580
  262.0 0.8 copy-start.5
  330.9 5.6 %copy-start.11 = (bf16[2048,32]{0,1:T(8,128)(2,1)S(1)}, bf16[2048,32]{0,1:T(8,128)(2,1)}, u32[]{:S(2)}) copy-start(bf16[2048,32]{0,1:T(8,128)(2,1)} %param.24) | copy-start | bytes 393220
  330.9 51.9 %all-to-all-start.2 = ((bf16[32,16,2048]{2,1,0:T(8,128)(2,1)}), bf16[32,16,2048]{2,1,0:T(8,128)(2,1)S(1)}, u32[]{:S(2)}, u32[]{:S(2)}) async-start(bf16[32,16,2048]{2,1,0:T(8,128)(2,1)} %bitcast.103), calls=%async_computation.2 | async-start | bytes 4194304 | tf_op jit(solution)/shard_map/all_to_all | solution.py:175
  389.8 3.8 copy-start.6
Sparse Core Ops, SparseCore 0:
  9.5 67.3 all-gather.6
  79.0 89.3 all-gather.4
  171.6 86.6 all-gather.8
  260.2 44.3 all-gather.10
